TPU v7x, 128 devices: a whole 4x4x4 slice. The times are simulated.
128 devices in a mesh: grp: 8 (over x_hi, z), vocab: 16 (over y, x_lo, core).
Axes of the slice: x: 4 (x_hi: 2, x_lo: 2; x = x_hi * 2 + x_lo), y: 4, z: 4, core: 2. Of those that a mesh axis runs over, the one named last changes fastest.
Arguments:
- hidden: bfloat16 [1024, 8192], P('grp', 'vocab')
- head_weight: bfloat16 [81920, 8192], P(('grp', 'vocab'))
- targets: int32 [1024], replicated, may hold values from 0 to 81919
- old_logprobs: float32 [1024], replicated
- loss_mask: int32 [1024], replicated, may hold values 0 or 1
- beam_lengths: int32 [128], replicated, may hold values from 1 to 24, 1024 in all
- beam_group: int32 [128], replicated, may hold values from 0 to 1, as said below
- rewards: float32 [128], replicated, may hold values from 0 to 1, as said below
Outputs:
- logprob: float32 [1024], replicated
- total_loss: float32 [], replicated
- head_grad: bfloat16 [81920, 8192], P(('grp', 'vocab'))
Inputs may be any that keep to these rules, and one draw needn't show every extreme that they name: `beam_group`: each of the 2 groups is named by exactly 64 beams. `rewards`: multiples of 1/8.
All inputs are finite; a program needn't handle non-finite values.
Results may differ from a plain program's by a relative error of at most 0.005.
Values may be sent and summed in bfloat16 or wider, within the bound.
No kernel may reach another device: no remote copies, remote signals or barrier semaphores. Data moves between devices by JAX's collectives and lax.ppermute only.
A program may use at most 128 MiB of HBM per device.

v0:
```python
import jax
import jax.numpy as jnp
from jax import lax
from jax.sharding import PartitionSpec as P

GROUP_BEAMS = 64


def policy_terms(logprob, old_logprobs, loss_mask, beam_lengths, beam_group, rewards):
    highest = lax.Precision.HIGHEST
    tok_count = logprob.shape[0]
    beam_count = beam_lengths.shape[0]
    group_count = beam_count // GROUP_BEAMS
    beam_ends = jnp.cumsum(beam_lengths)
    position = jnp.arange(tok_count, dtype=jnp.int32)
    beam_of = jnp.sum((position[:, None] >= beam_ends[None, :]).astype(jnp.int32), axis=1)
    token_beam = (beam_of[:, None] == jnp.arange(beam_count, dtype=jnp.int32)[None, :]).astype(
        jnp.float32
    )
    beam_onehot = (beam_group[:, None] == jnp.arange(group_count, dtype=jnp.int32)[None, :]).astype(
        jnp.float32
    )
    group_mean = jnp.dot(rewards, beam_onehot, precision=highest) / GROUP_BEAMS
    centred = rewards - jnp.dot(beam_onehot, group_mean, precision=highest)
    group_var = jnp.dot(centred * centred, beam_onehot, precision=highest) / GROUP_BEAMS
    advantage = centred / jnp.sqrt(jnp.dot(beam_onehot, group_var, precision=highest) + 1e-06)
    weight = loss_mask.astype(jnp.float32)
    counts = jnp.dot(weight, token_beam, precision=highest)
    token_adv = jnp.dot(token_beam, advantage, precision=highest)
    token_norm = jnp.dot(token_beam, jnp.maximum(counts, 1.0), precision=highest)
    ratios = jnp.exp(logprob - old_logprobs)
    clipped = jnp.clip(ratios, 0.8, 1.2)
    plain_term = ratios * token_adv
    bounded = clipped * token_adv
    token_share = weight / token_norm
    total_loss = -jnp.sum(token_share * jnp.minimum(plain_term, bounded))
    slopes = -token_share * jnp.where(plain_term <= bounded, plain_term, 0.0)
    return (total_loss, slopes)


def shards(
    hidden, head_weight, targets, old_logprobs, loss_mask, beam_lengths, beam_group, rewards
):
    token_block = lax.all_gather(hidden, "grp", axis=0, tiled=True)
    features = lax.all_gather(token_block, "vocab", axis=1, tiled=True)
    shard = head_weight.shape[0]
    offset = (lax.axis_index("grp") * lax.axis_size("vocab") + lax.axis_index("vocab")) * shard
    vocab_ids = offset + jnp.arange(shard, dtype=jnp.int32)
    logits = lax.dot_general(
        features, head_weight, (((1,), (1,)), ((), ())), preferred_element_type=jnp.float32
    )
    hits = targets[:, None] == vocab_ids[None, :]
    picked = jnp.sum(jnp.where(hits, logits, 0.0), axis=1)
    top = lax.pmax(jnp.max(logits, axis=1), ("grp", "vocab"))
    local_sum = jnp.sum(jnp.exp(logits - top[:, None]), axis=1)
    total, target_logit = lax.psum((local_sum, picked), ("grp", "vocab"))
    log_total = top + jnp.log(total)
    logprob = target_logit - log_total
    total_loss, slopes = policy_terms(
        logprob, old_logprobs, loss_mask, beam_lengths, beam_group, rewards
    )
    grads = (
        slopes[:, None] * (hits.astype(jnp.float32) - jnp.exp(logits - log_total[:, None]))
    ).astype(jnp.bfloat16)
    head_grad = lax.dot_general(
        grads, features, (((0,), (0,)), ((), ())), preferred_element_type=jnp.float32
    )
    return (logprob, total_loss, head_grad.astype(jnp.bfloat16))


def solution(mesh):
    in_specs = (P("grp", "vocab"), P(("grp", "vocab"), None), P(), P(), P(), P(), P(), P())
    out_specs = (P(), P(), P(("grp", "vocab"), None))
    return jax.shard_map(shards, mesh=mesh, in_specs=in_specs, out_specs=out_specs, check_vma=False)
```

profile of v0, /device:TPU:1, one launch (start us, length us, event | category | flops | bytes accessed | tf_op | source)
XLA Modules:
  0.0 327.0 jit_solution(1257413996547602422)
XLA Ops:
  7.2 0.0 all-gather.3.cloned.1.call-start
  7.2 0.7 all-gather.3.cloned.1.call-update
  7.9 0.0 all-gather.5.cloned.1.call-start
  7.9 50.5 %all-gather.3.cloned.1.call-done = bf16[1024,512]{1,0:T(8,128)(2,1)} async-done(((bf16[128,512]{1,0:T(8,128)(2,1)}), bf16[1024,512]{1,0:T(8,128)(2,1)}) %all-gather.3.cloned.1.call-update) | async-done | bytes 1048592 | tf_op jit(solution)/shard_map/all_gather | solution.py:44
  58.4 0.0 all-gather.5.cloned.1.call-update
  58.4 0.7 convert_element_type.17
  59.1 0.8 copy.13
  59.9 0.2 reduce-window.8
  60.1 0.1 reduce
  60.2 0.9 fusion.15
  61.0 0.9 fusion.13
  61.9 0.9 fusion.12
  62.9 0.9 fusion.17
  63.7 0.3 convert_reduce_fusion
  64.0 0.4 fusion.19
  64.4 0.5 fusion.21
  64.9 0.5 fusion.20
  65.3 87.1 %all-gather.5.cloned.1.call-done = bf16[1024,8192]{1,0:T(8,128)(2,1)} async-done(((bf16[1024,512]{1,0:T(8,128)(2,1)}), bf16[1024,8192]{1,0:T(8,128)(2,1)}) %all-gather.5.cloned.1.call-update) | async-done | bytes 16777232 | tf_op jit(solution)/shard_map/all_gather | solution.py:45
  152.4 16.3 %fusion.33 = (f32[1024]{0:T(1024)S(1)}, f32[1024,640]{0,1:T(8,128)S(1)}) fusion(bf16[1024,8192]{1,0:T(8,128)(2,1)} %all-gather.5.cloned.1.call-done, bf16[640,8192]{1,0:T(8,128)(2,1)} %param.9), kind=kOutput, calls=%fused_computation.52 | convolution fusion | flops 10738072576 | bytes 29888512 | tf_op jit(solution)/shard_map/dot_general | solution.py:49
  168.7 65.8 %pmax.7 = f32[1024]{0:T(1024)S(1)} all-reduce(f32[1024]{0:T(1024)S(1)} %get-tuple-element.10), channel_id=1, replica_groups=mesh['grp'=8,'vocab'=16] {'grp','vocab'}, use_global_device_ids=true, to_apply=%region_3.4 | all-reduce | flops 1024 | bytes 8192 | tf_op jit(solution)/shard_map/pmax | solution.py:54
  234.5 0.6 exponential_reduce_fusion
  235.2 63.1 %all-reduce = (f32[1024]{0:T(1024)S(1)}, f32[1024]{0:T(1024)S(1)}) all-reduce(f32[1024]{0:T(1024)S(1)} %get-tuple-element.4, f32[1024]{0:T(1024)S(1)} %get-tuple-element.3), channel_id=1, replica_groups=mesh['grp'=8,'vocab'=16] {'grp','vocab'}, use_global_device_ids=true, to_apply=%region_1.2 | all-reduce | flops 2048 | bytes 16384 | tf_op jit(solution)/shard_map/psum | solution.py:56
  298.2 0.6 multiply_reduce_fusion
  299.5 19.5 %convolution_convert_fusion = bf16[640,8192]{1,0:T(8,128)(2,1)} fusion(bf16[1024,8192]{1,0:T(8,128)(2,1)} %all-gather.5.cloned.1.call-done, f32[1024,640]{0,1:T(8,128)S(1)} %get-tuple-element.11, f32[1024]{0:T(1024)S(1)} %get-tuple-element.9, f32[1024]{0:T(1024)S(1)} %get-tuple-element.7, s32[1024]{0:T(1024)S(1)} %copy-done.3, s32[640]{0:T(1024)S(1)} %iota_add_fusion), kind=kOutput, calls=%fused_computation | convolution fusion | flops 10746593280 | bytes 29899264 | tf_op jit(solution)/shard_map/dot_general | solution.py:65
  (10 shorter events, 0.0 us)
Async XLA Ops:
  7.2 51.2 %all-gather.3.cloned.1.call-start = ((), (), s32[]{:S(2)}) async-start(), calls=%async_computation | async-start | bytes 1179648 | tf_op jit(solution)/shard_map/all_gather | solution.py:44
  7.9 144.5 %all-gather.5.cloned.1.call-start = ((), (), s32[]{:S(2)}) async-start(), calls=%async_computation.1 | async-start | bytes 17825792 | tf_op jit(solution)/shard_map/all_gather | solution.py:45
  65.3 169.2 %copy-start.3 = (s32[1024]{0:T(1024)S(1)}, s32[1024]{0:T(1024)}, u32[]{:S(2)}) copy-start(s32[1024]{0:T(1024)} %param.10) | copy-start | bytes 12292
  168.7 129.5 %copy-start = (s32[1024]{0:T(1024)S(1)}, s32[1024]{0:T(1024)}, u32[]{:S(2)}) copy-start(s32[1024]{0:T(1024)} %param.12) | copy-start | bytes 12292
  168.7 129.5 %copy-start.1 = (f32[1024]{0:T(1024)S(1)}, f32[1024]{0:T(1024)}, u32[]{:S(2)}) copy-start(f32[1024]{0:T(1024)} %param.11) | copy-start | bytes 12292
  298.2 20.8 %copy-start.2 = (f32[1024]{0:T(1024)}, f32[1024]{0:T(1024)S(1)}, u32[]{:S(2)}) copy-start(f32[1024]{0:T(1024)S(1)} %get-tuple-element.8) | copy-start | bytes 12292
Sparse Core Ops, SparseCore 0:
  10.3 48.0 all-gather.2
  60.1 92.3 all-gather.4
where the time goes:
time: 328 us; the launch traced here: 327 us
  waiting for transfers between devices  138 us (42%)
  blocking collectives  129 us (39%)
  matrix products  40.7 us (12%)
  between operations  15.9 us (5%)
    all_gather x1, waiting for transfers between devices, shards(): features = lax.all_gather(token_block, 'vocab', axis=1, tiled=True)  87.1 us
    pmax x1, blocking collectives, shards(): top = lax.pmax(jnp.max(logits, axis=1), ('grp', 'vocab'))  65.8 us
    psum x1, blocking collectives, shards(): total, target_logit = lax.psum((local_sum, picked), ('grp', 'vocab'))  63.1 us
    all_gather x1, waiting for transfers between devices, shards(): token_block = lax.all_gather(hidden, 'grp', axis=0, tiled=True)  50.5 us
    dot_general x1, matrix products, shards(): lax.dot_general(grads, features, (((0,), (0,)), ((), ())), preferred_elem...  19.5 us
    dot_general x1, matrix products, shards(): lax.dot_general(features, head_weight, (((1,), (1,)), ((), ())), preferre...  16.3 us
  transfers between devices with their start and end apart: 2, of which 2 were waited for; matrix products, arithmetic and copies ran while one was open for 2% of the time, Pallas kernels for 0%

commit v1 on v0

--- a/solution.py
+++ b/solution.py
@@ -2,8 +2,18 @@
 import jax.numpy as jnp
 from jax import lax
 from jax.sharding import PartitionSpec as P
+from jax.lax import all_to_all, axis_size
 
 GROUP_BEAMS = 64
+save_heads_on_mesh = lambda local_values, dev_axis: jnp.concatenate(
+    all_to_all(
+        jnp.stack([local_values] * axis_size(dev_axis)),
+        axis_name=dev_axis,
+        split_axis=0,
+        concat_axis=0,
+    ),
+    0,
+)
 
 
 def policy_terms(logprob, old_logprobs, loss_mask, beam_lengths, beam_group, rewards):
@@ -41,7 +51,7 @@
 def shards(
     hidden, head_weight, targets, old_logprobs, loss_mask, beam_lengths, beam_group, rewards
 ):
-    token_block = lax.all_gather(hidden, "grp", axis=0, tiled=True)
+    token_block = save_heads_on_mesh(hidden, "grp")
     features = lax.all_gather(token_block, "vocab", axis=1, tiled=True)
     shard = head_weight.shape[0]
     offset = (lax.axis_index("grp") * lax.axis_size("vocab") + lax.axis_index("vocab")) * shard

time: 328 us -> 298 us (0.909)
  waiting for transfers between devices: 138 us -> 88.3 us
  blocking collectives: 129 us -> 153 us
    all_gather x1 -> x0, waiting for transfers between devices: 50.5 us -> none  [shards(): token_block = lax.all_gather(hidden, 'grp', axis=0, tiled=True)]
    all_to_all x0 -> x1, blocking collectives: none -> 23.9 us  [all_to_all(jnp.stack([local_values] * axis_size(dev_axis)), axis_name=dev...]
  transfers between devices with their start and end apart: 2 -> 1, of which waited for: 2 -> 1; matrix products, arithmetic and copies ran while one was open for 2% -> 1% of each run, Pallas kernels for 0% -> 0%
where the time goes in v1:
time: 298 us
  blocking collectives  153 us (51%)
  waiting for transfers between devices  88.3 us (30%)
  matrix products  38 us (13%)
  between operations  16 us (5%)
    all_gather x1, waiting for transfers between devices, shards(): features = lax.all_gather(token_block, 'vocab', axis=1, tiled=True)  88.3 us
    pmax x1, blocking collectives, shards(): top = lax.pmax(jnp.max(logits, axis=1), ('grp', 'vocab'))  65.8 us
    psum x1, blocking collectives, shards(): total, target_logit = lax.psum((local_sum, picked), ('grp', 'vocab'))  63.1 us
    all_to_all x1, blocking collectives, all_to_all(jnp.stack([local_values] * axis_size(dev_axis)), axis_name=dev...  23.9 us
    dot_general x1, matrix products, shards(): lax.dot_general(grads, features, (((0,), (0,)), ((), ())), preferred_elem...  19.6 us
    dot_general x1, matrix products, shards(): lax.dot_general(features, head_weight, (((1,), (1,)), ((), ())), preferre...  16.3 us
  transfers between devices with their start and end apart: 1, of which 1 were waited for; matrix products, arithmetic and copies ran while one was open for 1% of the time, Pallas kernels for 0%

profile of v1, /device:TPU:1, one launch (start us, length us, event | category | flops | bytes accessed | tf_op | source)
XLA Modules:
  0.0 298.0 jit_solution(2307766915366226348)
XLA Ops:
  7.2 0.0 all-gather.2.cloned.1.call-start
  7.3 1.0 stack.2
  8.2 23.9 %all_to_all.5 = bf16[8,128,512]{2,1,0:T(8,128)(2,1)} all-to-all(bf16[8,128,512]{2,1,0:T(8,128)(2,1)S(1)} %stack.2), channel_id=1, replica_groups=mesh['grp'=8,'vocab'=16] {'grp'}, dimensions={0} | all-to-all | bytes 2097152 | tf_op jit(solution)/shard_map/all_to_all | solution.py:9
  32.1 0.0 all-gather.2.cloned.1.call-update
  32.2 0.1 copy.13
  32.3 0.2 reduce-window.8
  32.5 0.1 reduce
  32.6 0.2 fusion.15
  32.8 0.2 fusion.13
  33.0 0.3 fusion.12
  33.3 0.2 fusion.17
  33.5 0.3 convert_reduce_fusion
  33.8 0.4 fusion.19
  34.2 0.5 fusion.21
  34.6 0.5 fusion.20
  35.1 88.3 %all-gather.2.cloned.1.call-done = bf16[1024,8192]{1,0:T(8,128)(2,1)} async-done(((bf16[1024,512]{1,0:T(8,128)(2,1)}), bf16[1024,8192]{1,0:T(8,128)(2,1)}) %all-gather.2.cloned.1.call-update) | async-done | bytes 16777232 | tf_op jit(solution)/shard_map/all_gather | solution.py:55
  123.4 16.3 %fusion.33 = (f32[1024]{0:T(1024)S(1)}, f32[1024,640]{0,1:T(8,128)S(1)}) fusion(bf16[1024,8192]{1,0:T(8,128)(2,1)} %all-gather.2.cloned.1.call-done, bf16[640,8192]{1,0:T(8,128)(2,1)} %param.9), kind=kOutput, calls=%fused_computation.52 | convolution fusion | flops 10738072576 | bytes 29888512 | tf_op jit(solution)/shard_map/dot_general | solution.py:59
  139.7 0.0 copy-start.1
  139.7 65.8 %pmax.7 = f32[1024]{0:T(1024)S(1)} all-reduce(f32[1024]{0:T(1024)S(1)} %get-tuple-element.10), channel_id=1, replica_groups=mesh['grp'=8,'vocab'=16] {'grp','vocab'}, use_global_device_ids=true, to_apply=%region_3.4 | all-reduce | flops 1024 | bytes 8192 | tf_op jit(solution)/shard_map/pmax | solution.py:64
  205.5 0.6 exponential_reduce_fusion
  206.2 63.1 %all-reduce = (f32[1024]{0:T(1024)S(1)}, f32[1024]{0:T(1024)S(1)}) all-reduce(f32[1024]{0:T(1024)S(1)} %get-tuple-element.4, f32[1024]{0:T(1024)S(1)} %get-tuple-element.3), channel_id=1, replica_groups=mesh['grp'=8,'vocab'=16] {'grp','vocab'}, use_global_device_ids=true, to_apply=%region_1.2 | all-reduce | flops 2048 | bytes 16384 | tf_op jit(solution)/shard_map/psum | solution.py:66
  269.2 0.0 copy-start.2
  269.2 0.6 multiply_reduce_fusion
  270.5 19.6 %convolution_convert_fusion = bf16[640,8192]{1,0:T(8,128)(2,1)} fusion(bf16[1024,8192]{1,0:T(8,128)(2,1)} %all-gather.2.cloned.1.call-done, f32[1024,640]{0,1:T(8,128)S(1)} %get-tuple-element.11, f32[1024]{0:T(1024)S(1)} %get-tuple-element.9, f32[1024]{0:T(1024)S(1)} %get-tuple-element.7, s32[1024]{0:T(1024)S(1)} %copy-done.3, s32[640]{0:T(1024)S(1)} %iota_add_fusion), kind=kOutput, calls=%fused_computation | convolution fusion | flops 10746593280 | bytes 29899264 | tf_op jit(solution)/shard_map/dot_general | solution.py:75
  (15 shorter events, 0.0 us)
Async XLA Ops:
  7.2 25.0 %copy-start = (s32[1024]{0:T(1024)S(1)}, s32[1024]{0:T(1024)}, u32[]{:S(2)}) copy-start(s32[1024]{0:T(1024)} %param.12) | copy-start | bytes 12292
  7.2 25.0 %copy-start.4 = (s32[128]{0:T(128)S(1)}, s32[128]{0:T(128)}, u32[]{:S(2)}) copy-start(s32[128]{0:T(128)} %param.13) | copy-start | bytes 1540
  7.2 25.4 %copy-start.6 = (s32[128]{0:T(128)S(1)}, s32[128]{0:T(128)}, u32[]{:S(2)}) copy-start(s32[128]{0:T(128)} %param.14) | copy-start | bytes 1540
  7.2 25.4 %copy-start.5 = (f32[128]{0:T(128)S(1)}, f32[128]{0:T(128)}, u32[]{:S(2)}) copy-start(f32[128]{0:T(128)} %param.15) | copy-start | bytes 1540
  7.2 116.2 %all-gather.2.cloned.1.call-start = ((), (), s32[]{:S(2)}) async-start(), calls=%async_computation.1 | async-start | bytes 17825792 | tf_op jit(solution)/shard_map/all_gather | solution.py:55
  35.1 170.4 %copy-start.3 = (s32[1024]{0:T(1024)S(1)}, s32[1024]{0:T(1024)}, u32[]{:S(2)}) copy-start(s32[1024]{0:T(1024)} %param.10) | copy-start | bytes 12292
  139.7 129.5 %copy-start.1 = (f32[1024]{0:T(1024)S(1)}, f32[1024]{0:T(1024)}, u32[]{:S(2)}) copy-start(f32[1024]{0:T(1024)} %param.11) | copy-start | bytes 12292
  269.2 20.8 %copy-start.2 = (f32[1024]{0:T(1024)}, f32[1024]{0:T(1024)S(1)}, u32[]{:S(2)}) copy-start(f32[1024]{0:T(1024)S(1)} %get-tuple-element.8) | copy-start | bytes 12292
Sparse Core Ops, SparseCore 0:
  32.3 91.1 all-gather.1
